TPU v7x, 256 devices: a whole 4x4x8 slice. The times are simulated.
256 devices in a mesh: leaf: 2 (over core), row: 8 (over z), col: 16 (over y, x).
Axes of the slice: x: 4, y: 4, z: 8, core: 2. Of those that a mesh axis runs over, the one named last changes fastest.
Arguments:
- front: float32 [2, 8, 8, 128, 4, 16, 128], P('leaf', None, 'row', None, None, 'col'), as said below
- parent: float32 [4, 2, 8, 128, 4, 16, 128], P(None, 'leaf', 'row', None, None, 'col'), may hold values from -0.2 to 0.2
- tile_map: int32 [2, 56], replicated, may hold values from 0 to 63, as said below
- col_shift: int32 [4], replicated, may hold values from 0 to 7
Outputs:
- factored: float32 [2, 8, 8, 128, 4, 16, 128], P('leaf', None, 'row', None, None, 'col')
- new_parent: float32 [4, 2, 8, 128, 4, 16, 128], P(None, 'leaf', 'row', None, None, 'col')
Inputs may be any that keep to these rules, and one draw needn't show every extreme that they name: For each leaf the 8192 x 8192 matrix read from front is symmetric positive definite. Entry [l, e] names the parent tile joined by tile 8 + e of child l; no row repeats a value. The parent tile q = tile_map[l, e] has (q mod 16 + col_shift[q // 16]) mod 16 equal to (8 + e) mod 16. Among the tiles of one child whose indices are equal mod 8, at most 1 have parent tiles equal mod 16.
All inputs are finite; a program needn't handle non-finite values.
Results may differ from a plain program's by a relative error of at most 0.0001.
Values sent between devices are 32-bit elements; how exact they have to be, the bound alone decides.
No kernel may reach another device: no remote copies, remote signals or barrier semaphores. Data moves between devices by JAX's collectives and lax.ppermute only.
A program may use at most 128 MiB of HBM per device.

v0:
```python
import jax
import jax.numpy as jnp
from jax import lax
from jax.sharding import PartitionSpec as P

TILE = 128
PB = 512
PANELS = 2
NPIV = 1024
HIGHEST = lax.Precision.HIGHEST


def spread(value, axis, source):
    kept = jnp.where(lax.axis_index(axis) == source, value, 0).astype(value.dtype)
    return lax.psum(kept, axis)


def update_slots(working, next_rows, column_factor, slot_low, slot_high):
    product = jnp.einsum(
        "atp,bsp->atbs",
        next_rows,
        column_factor,
        precision=HIGHEST,
        preferred_element_type=jnp.float32,
    )
    return working.at[:, :, slot_low:slot_high, :].add(-product)


def per_device(front, parent, tile_map, col_shift):
    leaf_count = lax.axis_size("leaf")
    row_count = lax.axis_size("row")
    col_count = lax.axis_size("col")
    leaf_index = lax.axis_index("leaf")
    row_index = lax.axis_index("row")
    col_index = lax.axis_index("col")
    local_front = front[0, :, 0, :, :, 0, :]
    row_slots = local_front.shape[0]
    col_slots = local_front.shape[2]
    pivot_tiles = NPIV // TILE
    assert pivot_tiles == row_count and pivot_tiles <= col_count
    row_tiles = jnp.arange(row_slots, dtype=jnp.int32) * row_count + row_index
    col_tiles = jnp.arange(col_slots, dtype=jnp.int32) * col_count + col_index
    working = local_front
    top_rows = lax.all_gather(working[0], "row", axis=0, tiled=False)
    column_panel = top_rows.transpose(2, 3, 0, 1).reshape(col_slots, TILE, NPIV)
    first_cols = lax.all_gather(working[:, :, 0, :], "col", axis=0, tiled=False)
    row_panel = first_cols[:pivot_tiles].transpose(1, 2, 0, 3).reshape(row_slots, TILE, NPIV)
    diagonal_block = lax.all_gather(row_panel[0], "row", axis=0, tiled=True)
    lower_factor = jnp.linalg.cholesky(diagonal_block)
    stacked = jnp.concatenate(
        [row_panel[1:].reshape(-1, NPIV), column_panel.reshape(-1, NPIV)], axis=0
    )
    solved = lax.linalg.triangular_solve(
        lower_factor, stacked, left_side=False, lower=True, transpose_a=True
    )
    trailing_rows = (row_slots - 1) * TILE
    row_factor = solved[:trailing_rows].reshape(row_slots - 1, TILE, NPIV)
    column_factor = solved[trailing_rows:].reshape(col_slots, TILE, NPIV)
    column_factor = jnp.where((col_tiles >= pivot_tiles)[:, None, None], column_factor, 0.0)
    product = jnp.einsum(
        "atk,bsk->atbs",
        row_factor,
        column_factor,
        precision=HIGHEST,
        preferred_element_type=jnp.float32,
    )
    trailing = working[1:] - product
    own_col = jnp.minimum(col_index, pivot_tiles - 1)
    row_factor_cols = lax.dynamic_slice_in_dim(row_factor, own_col * TILE, TILE, 2)
    is_factor_col = (col_tiles < pivot_tiles)[None, None, :, None]
    trailing = jnp.where(is_factor_col, row_factor_cols[:, :, None, :], trailing)
    diag_rows = lax.dynamic_slice_in_dim(lower_factor, row_index * TILE, TILE, 0)
    diag_tile = lax.dynamic_slice_in_dim(diag_rows, own_col * TILE, TILE, 1)
    local_ids = jnp.arange(TILE, dtype=jnp.int32)
    global_row = row_index * TILE + local_ids[:, None]
    global_col = own_col * TILE + local_ids[None, :]
    diag_tile = jnp.where(global_row >= global_col, diag_tile, 0.0)
    top = jnp.where(is_factor_col[0], diag_tile[:, None, :], 0.0)
    top = jnp.broadcast_to(top, working[0].shape)
    working = jnp.concatenate([top[None], trailing], axis=0)
    factored = working.reshape(front.shape)
    contribution = jnp.where((col_tiles >= pivot_tiles)[None, None, :, None], working, 0.0)
    contrib_count = tile_map.shape[1]
    entry_ids = jnp.arange(contrib_count, dtype=jnp.int32)
    own_map = lax.dynamic_index_in_dim(tile_map, leaf_index, 0, keepdims=False)
    row_match = (row_tiles - pivot_tiles)[:, None] == entry_ids[None, :]
    row_targets = jnp.sum(jnp.where(row_match, own_map[None, :], 0), axis=1)
    row_valid = row_tiles >= pivot_tiles
    owner_count = leaf_count * row_count
    destination = row_targets % owner_count
    parent_row_slot = row_targets // owner_count
    slot_ids = jnp.arange(row_slots, dtype=jnp.int32)
    same_before = (
        (destination[None, :] == destination[:, None])
        & row_valid[None, :]
        & (slot_ids[None, :] < slot_ids[:, None])
    )
    rank_in_dest = jnp.sum(same_before.astype(jnp.int32), axis=1)
    capacity = (col_slots + row_count - 1) // row_count
    owner_ids = jnp.arange(owner_count, dtype=jnp.int32)
    capacity_ids = jnp.arange(capacity, dtype=jnp.int32)
    selection = (
        row_valid[None, None, :]
        & (destination[None, None, :] == owner_ids[:, None, None])
        & (rank_in_dest[None, None, :] == capacity_ids[None, :, None])
    )
    flattened = contribution.reshape(row_slots, -1)
    send_buffer = jnp.einsum(
        "oka,ax->okx",
        selection.astype(jnp.float32),
        flattened,
        precision=HIGHEST,
        preferred_element_type=jnp.float32,
    )
    chosen_slot = jnp.sum(jnp.where(selection, parent_row_slot[None, None, :], 0), axis=2)
    send_slots = jnp.where(jnp.any(selection, axis=2), chosen_slot, -1)
    received, received_slots = (
        lax.all_to_all(send_buffer, ("leaf", "row"), split_axis=0, concat_axis=0, tiled=True),
        lax.all_to_all(send_slots, ("leaf", "row"), split_axis=0, concat_axis=0, tiled=True),
    )
    received = received.reshape(leaf_count, row_count, capacity, -1)
    received_slots = received_slots.reshape(leaf_count, row_count, capacity)
    parent_local = parent[:, 0, 0, :, :, 0, :]
    parent_rows = parent_local.shape[0]
    parent_cols = parent_local.shape[2]
    row_place = (
        received_slots[None] == jnp.arange(parent_rows, dtype=jnp.int32)[:, None, None, None]
    ).astype(jnp.float32)
    by_leaf = jnp.einsum(
        "slrk,lrkx->slx", row_place, received, precision=HIGHEST, preferred_element_type=jnp.float32
    )
    by_leaf = by_leaf.reshape(parent_rows, leaf_count, TILE, col_slots, TILE)
    col_match = (col_tiles - pivot_tiles)[:, None] == entry_ids[None, :]
    col_targets = jnp.sum(jnp.where(col_match[None], tile_map[:, None, :], 0), axis=2)
    col_valid = col_tiles >= pivot_tiles
    parent_slot_ids = jnp.arange(parent_cols, dtype=jnp.int32)
    col_place = (
        col_valid[None, None, :]
        & (col_targets[:, None, :] // col_count == parent_slot_ids[None, :, None])
    ).astype(jnp.float32)
    assembled = jnp.einsum(
        "sltbv,lub->stuv", by_leaf, col_place, precision=HIGHEST, preferred_element_type=jnp.float32
    )
    new_parent = (parent_local + assembled).reshape(parent.shape)
    return (factored, new_parent)


def solution(mesh):
    return jax.shard_map(
        per_device,
        mesh=mesh,
        in_specs=(
            P("leaf", None, "row", None, None, "col", None),
            P(None, "leaf", "row", None, None, "col", None),
            P(),
            P(),
        ),
        out_specs=(
            P("leaf", None, "row", None, None, "col", None),
            P(None, "leaf", "row", None, None, "col", None),
        ),
        check_vma=False,
    )
```

profile of v0, /device:TPU:1, one launch (start us, length us, event | category | flops | bytes accessed | tf_op | source)
XLA Modules:
  0.0 730.9 jit_solution(1884247141406783807)
XLA Ops:
  12.2 78.9 %all-gather.8.cloned.1.call-done = f32[128,128,1,128]{3,1,2,0:T(8,128)} async-done(((f32[8,128,1,128]{3,1,2,0:T(8,128)}), f32[128,128,1,128]{3,1,2,0:T(8,128)}) %all-gather.8.cloned.1.call-update) | async-done | bytes 8388624 | tf_op jit(solution)/shard_map/all_gather | solution.py:46
  107.8 22.4 %all-gather.10.cloned.1.call-done = f32[8,1,1,128,4,1,128]{6,3,5,4,2,1,0:T(8,128)} async-done(((f32[1,1,1,128,4,1,128]{6,3,5,4,2,1,0:T(8,128)}), f32[8,1,1,128,4,1,128]{6,3,5,4,2,1,0:T(8,128)}) %all-gather.10.cloned.1.call-update) | async-done | bytes 2097168 | tf_op jit(solution)/shard_map/all_gather | solution.py:44
  139.0 55.7 %all-gather.6.cloned.1.call-done = f32[1024,1024]{0,1:T(8,128)} async-done(((f32[128,1024]{0,1:T(8,128)}), f32[1024,1024]{0,1:T(8,128)}) %all-gather.6.cloned.1.call-update) | async-done | bytes 4194320 | tf_op jit(solution)/shard_map/all_gather | solution.py:48
  206.6 11.7 %cholesky.223 = f32[128,128]{1,0:T(8,128)S(1)} custom-call(f32[128,128]{1,0:T(8,128)S(1)} %cholesky.580), custom_call_target="Cholesky" | custom-call | tf_op jit(solution)/shard_map/jit(cholesky)/cholesky | solution.py:49
  218.4 9.8 %custom-call.62 = f32[1,128,128]{1,2,0:T(8,128)S(1)} custom-call(f32[1,128,128]{2,1,0:T(8,128)S(1)} %get-tuple-element.80), custom_call_target="InvertDiagBlocksLowerTriangular" | custom-call | tf_op jit(solution)/shard_map/jit(cholesky)/cholesky | solution.py:49
  234.6 11.9 %cholesky.244 = f32[128,128]{1,0:T(8,128)S(1)} custom-call(f32[128,128]{1,0:T(8,128)S(1)} %cholesky.584), custom_call_target="Cholesky" | custom-call | tf_op jit(solution)/shard_map/jit(cholesky)/cholesky | solution.py:49
  247.2 9.8 %custom-call.63 = f32[1,128,128]{1,2,0:T(8,128)S(1)} custom-call(f32[1,128,128]{2,1,0:T(8,128)S(1)} %get-tuple-element.77), custom_call_target="InvertDiagBlocksLowerTriangular" | custom-call | tf_op jit(solution)/shard_map/jit(cholesky)/cholesky | solution.py:49
  260.3 11.7 %cholesky.468 = f32[128,128]{1,0:T(8,128)S(1)} custom-call(f32[128,128]{1,0:T(8,128)S(1)} %cholesky.589), custom_call_target="Cholesky" | custom-call | tf_op jit(solution)/shard_map/jit(cholesky)/cholesky | solution.py:49
  273.3 9.8 %custom-call.64 = f32[1,128,128]{1,2,0:T(8,128)S(1)} custom-call(f32[1,128,128]{2,1,0:T(8,128)S(1)} %get-tuple-element.74), custom_call_target="InvertDiagBlocksLowerTriangular" | custom-call | tf_op jit(solution)/shard_map/jit(cholesky)/cholesky | solution.py:49
  286.7 12.1 %cholesky.487 = f32[128,128]{1,0:T(8,128)S(1)} custom-call(f32[128,128]{1,0:T(8,128)S(1)} %cholesky.594), custom_call_target="Cholesky" | custom-call | tf_op jit(solution)/shard_map/jit(cholesky)/cholesky | solution.py:49
  300.0 9.8 %custom-call.65 = f32[1,128,128]{1,2,0:T(8,128)S(1)} custom-call(f32[1,128,128]{2,1,0:T(8,128)S(1)} %get-tuple-element.71), custom_call_target="InvertDiagBlocksLowerTriangular" | custom-call | tf_op jit(solution)/shard_map/jit(cholesky)/cholesky | solution.py:49
  313.3 11.7 %cholesky.506 = f32[128,128]{1,0:T(8,128)S(1)} custom-call(f32[128,128]{1,0:T(8,128)S(1)} %cholesky.599), custom_call_target="Cholesky" | custom-call | tf_op jit(solution)/shard_map/jit(cholesky)/cholesky | solution.py:49
  326.4 9.9 %custom-call.66 = f32[1,128,128]{1,2,0:T(8,128)S(1)} custom-call(f32[1,128,128]{2,1,0:T(8,128)S(1)} %get-tuple-element.68), custom_call_target="InvertDiagBlocksLowerTriangular" | custom-call | tf_op jit(solution)/shard_map/jit(cholesky)/cholesky | solution.py:49
  339.6 11.7 %cholesky.526 = f32[128,128]{1,0:T(8,128)S(1)} custom-call(f32[128,128]{1,0:T(8,128)S(1)} %cholesky.604), custom_call_target="Cholesky" | custom-call | tf_op jit(solution)/shard_map/jit(cholesky)/cholesky | solution.py:49
  352.6 9.8 %custom-call.67 = f32[1,128,128]{1,2,0:T(8,128)S(1)} custom-call(f32[1,128,128]{2,1,0:T(8,128)S(1)} %get-tuple-element.65), custom_call_target="InvertDiagBlocksLowerTriangular" | custom-call | tf_op jit(solution)/shard_map/jit(cholesky)/cholesky | solution.py:49
  365.4 11.9 %cholesky.546 = f32[128,128]{1,0:T(8,128)S(1)} custom-call(f32[128,128]{1,0:T(8,128)S(1)} %cholesky.609), custom_call_target="Cholesky" | custom-call | tf_op jit(solution)/shard_map/jit(cholesky)/cholesky | solution.py:49
  378.7 9.8 %custom-call.68 = f32[1,128,128]{1,2,0:T(8,128)S(1)} custom-call(f32[1,128,128]{2,1,0:T(8,128)S(1)} %get-tuple-element.62), custom_call_target="InvertDiagBlocksLowerTriangular" | custom-call | tf_op jit(solution)/shard_map/jit(cholesky)/cholesky | solution.py:49
  391.1 11.7 %cholesky.564 = f32[128,128]{1,0:T(8,128)S(1)} custom-call(f32[128,128]{1,0:T(8,128)S(1)} %convolution_subtract_fusion.12), custom_call_target="Cholesky" | custom-call | tf_op jit(solution)/shard_map/jit(cholesky)/cholesky | solution.py:49
  416.4 23.3 %while.1 = (s32[]{:T(128)}, f32[1024,1024]{1,0:T(8,128)}, s32[8,2]{0,1:T(2,128)S(1)}, f32[8,128,128]{2,1,0:T(8,128)S(1)}, s32[]{:T(128)}) while((s32[]{:T(128)}, f32[1024,1024]{1,0:T(8,128)}, s32[8,2]{0,1:T(2,128)S(1)}, f32[8,128,128]{2,1,0:T(8,128)S(1)}, s32[]{:T(128)}) %tuple.72), condition=%wide.while_cond, body=%wide.while_body.sunk | while | flops 2 | bytes 131189 | solution.py:53
  439.7 79.0 %custom-call.69 = f32[8,128,128]{1,2,0:T(8,128)S(1)} custom-call(f32[8,128,128]{2,1,0:T(8,128)S(1)} %get-tuple-element.9), custom_call_target="InvertDiagBlocksLowerTriangular" | custom-call | tf_op jit(solution)/shard_map/triangular_solve | solution.py:53
  559.7 10.1 %convolution_subtract_fusion.4 = f32[1408,128]{1,0:T(8,128)S(1)} fusion(f32[1408,896]{0,1:T(8,128)S(1)} %get-tuple-element.34, f32[1408,1024]{1,0:T(8,128)} %bitcast_dynamic-update-slice_fusion.2, f32[1024,1024]{1,0:T(8,128)} %get-tuple-element.146), kind=kOutput, calls=%fused_computation.26 | convolution fusion | flops 1937948672 | bytes 6946816 | tf_op jit(solution)/shard_map/triangular_solve | solution.py:53
  582.2 9.0 %fusion.23 = f32[7,128,4,128]{3,1,2,0:T(8,128)S(1)} fusion(f32[1,8,1,128,4,1,128]{6,3,4,1,5,2,0:T(8,128)} %copy-done.2, f32[7,128,1024,1]{2,1,3,0:T(8,128)} %bitcast.180, f32[4,128,1024,1]{2,1,0,3:T(8,128)} %bitcast.183, f32[7,128,128]{2,1,0:T(8,128)S(1)} %constant_dynamic-slice_fusion.2, pred[4]{0:T(512)(128)(4,1)S(1)} %get-tuple-element.92), kind=kOutput, calls=%fused_computation.42 | convolution fusion | flops 5638062080 | bytes 9895940 | tf_op jit(solution)/shard_map/atk,bsk->atbs/dot_general | solution.py:60
  607.5 10.2 %all-to-all-start = ((f32[16,1,65536]{2,1,0:T(1,128)}), f32[16,1,65536]{2,1,0:T(1,128)}, u32[]{:S(2)}, u32[]{:S(2)}) async-start(f32[16,1,65536]{2,1,0:T(1,128)} %copy.66), calls=%async_computation | async-start | bytes 8388608 | tf_op jit(solution)/shard_map/all_to_all | solution.py:118
  622.2 88.3 %all-to-all-done = f32[16,1,65536]{2,1,0:T(1,128)} async-done(((f32[16,1,65536]{2,1,0:T(1,128)}), f32[16,1,65536]{2,1,0:T(1,128)}, u32[]{:S(2)}, u32[]{:S(2)}) %all-to-all-start) | async-done | bytes 4194336 | tf_op jit(solution)/shard_map/all_to_all | solution.py:118
  (151 shorter events, 194.7 us)
Async XLA Ops:
  7.2 4.2 slice-start.1
  7.2 83.8 %all-gather.8.cloned.1.call-start = ((), (), s32[]{:S(2)}) async-start(), calls=%async_computation.3 | async-start | bytes 8912896 | tf_op jit(solution)/shard_map/all_gather | solution.py:46
  9.1 1.3 copy-start.2
  11.3 118.9 %all-gather.10.cloned.1.call-start = ((), (), s32[]{:S(2)}) async-start(), calls=%async_computation.4 | async-start | bytes 2359296 | tf_op jit(solution)/shard_map/all_gather | solution.py:44
  12.1 182.5 %all-gather.6.cloned.1.call-start = ((), (), s32[]{:S(2)}) async-start(), calls=%async_computation.2 | async-start | bytes 4718592 | tf_op jit(solution)/shard_map/all_gather | solution.py:48
  91.0 2.2 slice-start
  93.2 5.4 copy-start.4
  95.6 1.9 copy-start
  99.9 507.6 %all-to-all-start.1 = ((s32[16,1,1]{2,1,0:T(1,128)}), s32[16,1,1]{2,1,0:T(1,128)S(1)}, u32[]{:S(2)}, u32[]{:S(2)}) async-start(s32[16,1,1]{2,1,0:T(1,128)} %copy.67), calls=%async_computation.1 | async-start | bytes 16384 | tf_op jit(solution)/shard_map/all_to_all | solution.py:119
  204.6 2.0 copy-start.1
  607.5 103.0 %all-to-all-start = ((f32[16,1,65536]{2,1,0:T(1,128)}), f32[16,1,65536]{2,1,0:T(1,128)}, u32[]{:S(2)}, u32[]{:S(2)}) async-start(f32[16,1,65536]{2,1,0:T(1,128)} %copy.66), calls=%async_computation | async-start | bytes 8388608 | tf_op jit(solution)/shard_map/all_to_all | solution.py:118
  622.2 99.2 %copy-start.3 = (f32[4,1,1,128,4,1,128]{6,5,4,3,2,1,0:T(1,128)S(1)}, f32[4,1,1,128,4,1,128]{6,5,4,3,2,1,0:T(1,128)}, u32[]{:S(2)}) copy-start(f32[4,1,1,128,4,1,128]{6,5,4,3,2,1,0:T(1,128)} %param.5) | copy-start | bytes 3145732
Sparse Core Ops, SparseCore 0:
  11.4 79.5 all-gather.7
  92.8 37.3 all-gather.9
  132.5 62.1 all-gather.5
where the time goes:
time: 737 us; the launch traced here: 731 us
  other arithmetic  266 us (36%)
  waiting for transfers between devices  245 us (33%)
  matrix products  98.3 us (13%)
  local copies, waits for them, and re-layouts  84.2 us (11%)
  between operations  19.4 us (3%)
  starting transfers between devices  18 us (2%)
    another operation x30, other arithmetic, per_device(): lower_factor = jnp.linalg.cholesky(diagonal_block)  172 us
    all_to_all x1, waiting for transfers between devices, per_device(): lax.all_to_all(send_buffer, ('leaf', 'row'), split_axis=0, concat_axis=0,...  88.3 us
    another operation x3, other arithmetic, per_device(): lax.linalg.triangular_solve(lower_factor, stacked, left_side=False, lower...  85.7 us
    all_gather x1, waiting for transfers between devices, per_device(): first_cols = lax.all_gather(working[:, :, 0, :], 'col', axis=0, tiled=False)  78.9 us
    all_gather x1, waiting for transfers between devices, per_device(): diagonal_block = lax.all_gather(row_panel[0], 'row', axis=0, tiled=True)  55.7 us
    another operation x15, matrix products, per_device(): lax.linalg.triangular_solve(lower_factor, stacked, left_side=False, lower...  51.9 us
    another operation x24, local copies, waits for them, and re-layouts  23.1 us
    another operation x14, matrix products, per_device(): lower_factor = jnp.linalg.cholesky(diagonal_block)  23.1 us
  transfers between devices with their start and end apart: 5, of which 4 were waited for; matrix products, arithmetic and copies ran while one was open for 58% of the time, Pallas kernels for 0%

commit v1 on v0

--- a/solution.py
+++ b/solution.py
@@ -8,6 +8,12 @@
 PANELS = 2
 NPIV = 1024
 HIGHEST = lax.Precision.HIGHEST
+
+
+def gather_by_exchange(x, axis, dim):
+    devices = lax.axis_size(axis)
+    repeats = [devices if d == dim else 1 for d in range(x.ndim)]
+    return lax.all_to_all(jnp.tile(x, repeats), axis, split_axis=dim, concat_axis=dim, tiled=True)
 
 
 def spread(value, axis, source):
@@ -45,7 +51,7 @@
     column_panel = top_rows.transpose(2, 3, 0, 1).reshape(col_slots, TILE, NPIV)
     first_cols = lax.all_gather(working[:, :, 0, :], "col", axis=0, tiled=False)
     row_panel = first_cols[:pivot_tiles].transpose(1, 2, 0, 3).reshape(row_slots, TILE, NPIV)
-    diagonal_block = lax.all_gather(row_panel[0], "row", axis=0, tiled=True)
+    diagonal_block = gather_by_exchange(row_panel[0], "row", 0)
     lower_factor = jnp.linalg.cholesky(diagonal_block)
     stacked = jnp.concatenate(
         [row_panel[1:].reshape(-1, NPIV), column_panel.reshape(-1, NPIV)], axis=0

time: 737 us -> 771 us (1.046)
  waiting for transfers between devices: 245 us -> 271 us
    all_gather x1, waiting for transfers between devices: 22.4 us -> 85.5 us  [per_device(): top_rows = lax.all_gather(working[0], 'row', axis=0, tiled=False)]
    all_gather x1 -> x0, waiting for transfers between devices: 55.7 us -> none  [per_device(): diagonal_block = lax.all_gather(row_panel[0], 'row', axis=0, tiled=True)]
    all_to_all x0 -> x1, waiting for transfers between devices: none -> 17.6 us  [gather_by_exchange(): lax.all_to_all(jnp.tile(x, repeats), axis, split_axis=dim, concat_axis=di...]
    all_to_all x0 -> x2, local copies, waits for them, and re-layouts: none -> 10.2 us  [gather_by_exchange(): lax.all_to_all(jnp.tile(x, repeats), axis, split_axis=dim, concat_axis=di...]
    another operation x24 -> x25, local copies, waits for them, and re-layouts: 23.1 us -> 25.5 us
  transfers between devices with their start and end apart: 5 -> 5, of which waited for: 4 -> 4; matrix products, arithmetic and copies ran while one was open for 58% -> 56% of each run, Pallas kernels for 0% -> 0%
where the time goes in v1:
time: 771 us; the launch traced here: 765 us
  waiting for transfers between devices  271 us (35%)
  other arithmetic  265 us (34%)
  matrix products  98.5 us (13%)
  local copies, waits for them, and re-layouts  90.6 us (12%)
  between operations  21.1 us (3%)
  starting transfers between devices  18.3 us (2%)
    another operation x30, other arithmetic, per_device(): lower_factor = jnp.linalg.cholesky(diagonal_block)  172 us
    all_to_all x1, waiting for transfers between devices, per_device(): lax.all_to_all(send_buffer, ('leaf', 'row'), split_axis=0, concat_axis=0,...  88.1 us
    another operation x3, other arithmetic, per_device(): lax.linalg.triangular_solve(lower_factor, stacked, left_side=False, lower...  85.7 us
    all_gather x1, waiting for transfers between devices, per_device(): top_rows = lax.all_gather(working[0], 'row', axis=0, tiled=False)  85.5 us
    all_gather x1, waiting for transfers between devices, per_device(): first_cols = lax.all_gather(working[:, :, 0, :], 'col', axis=0, tiled=False)  79.7 us
    another operation x15, matrix products, per_device(): lax.linalg.triangular_solve(lower_factor, stacked, left_side=False, lower...  51.9 us
    another operation x14, matrix products, per_device(): lower_factor = jnp.linalg.cholesky(diagonal_block)  23.2 us
    another operation x24, local copies, waits for them, and re-layouts  23.1 us
  transfers between devices with their start and end apart: 5, of which 4 were waited for; matrix products, arithmetic and copies ran while one was open for 56% of the time, Pallas kernels for 0%

profile of v1, /device:TPU:1, one launch (start us, length us, event | category | flops | bytes accessed | tf_op | source)
XLA Modules:
  0.0 764.6 jit_solution(17324432708847414662)
XLA Ops:
  12.1 79.7 %all-gather.5.cloned.1.call-done = f32[128,128,1,128]{3,1,2,0:T(8,128)} async-done(((f32[8,128,1,128]{3,1,2,0:T(8,128)}), f32[128,128,1,128]{3,1,2,0:T(8,128)}) %all-gather.5.cloned.1.call-update) | async-done | bytes 8388624 | tf_op jit(solution)/shard_map/all_gather | solution.py:52
  107.9 85.5 %all-gather.7.cloned.1.call-done = f32[8,1,1,128,4,1,128]{6,3,5,4,2,1,0:T(8,128)} async-done(((f32[1,1,1,128,4,1,128]{6,3,5,4,2,1,0:T(8,128)}), f32[8,1,1,128,4,1,128]{6,3,5,4,2,1,0:T(8,128)}) %all-gather.7.cloned.1.call-update) | async-done | bytes 2097168 | tf_op jit(solution)/shard_map/all_gather | solution.py:50
  204.4 17.6 %all-to-all-done = f32[8,128,1024]{1,2,0:T(8,128)} async-done(((f32[8,128,1024]{1,2,0:T(8,128)}), f32[8,128,1024]{1,2,0:T(8,128)}, u32[]{:S(2)}, u32[]{:S(2)}) %all-to-all-start) | async-done | bytes 4194336 | tf_op jit(solution)/shard_map/all_to_all | solution.py:16
  242.2 11.7 %cholesky.223 = f32[128,128]{1,0:T(8,128)S(1)} custom-call(f32[128,128]{1,0:T(8,128)S(1)} %cholesky.580), custom_call_target="Cholesky" | custom-call | tf_op jit(solution)/shard_map/jit(cholesky)/cholesky | solution.py:55
  254.0 9.8 %custom-call.62 = f32[1,128,128]{1,2,0:T(8,128)S(1)} custom-call(f32[1,128,128]{2,1,0:T(8,128)S(1)} %get-tuple-element.82), custom_call_target="InvertDiagBlocksLowerTriangular" | custom-call | tf_op jit(solution)/shard_map/jit(cholesky)/cholesky | solution.py:55
  270.2 11.7 %cholesky.244 = f32[128,128]{1,0:T(8,128)S(1)} custom-call(f32[128,128]{1,0:T(8,128)S(1)} %cholesky.584), custom_call_target="Cholesky" | custom-call | tf_op jit(solution)/shard_map/jit(cholesky)/cholesky | solution.py:55
  282.6 10.0 %custom-call.63 = f32[1,128,128]{1,2,0:T(8,128)S(1)} custom-call(f32[1,128,128]{2,1,0:T(8,128)S(1)} %get-tuple-element.79), custom_call_target="InvertDiagBlocksLowerTriangular" | custom-call | tf_op jit(solution)/shard_map/jit(cholesky)/cholesky | solution.py:55
  295.9 11.7 %cholesky.468 = f32[128,128]{1,0:T(8,128)S(1)} custom-call(f32[128,128]{1,0:T(8,128)S(1)} %cholesky.589), custom_call_target="Cholesky" | custom-call | tf_op jit(solution)/shard_map/jit(cholesky)/cholesky | solution.py:55
  308.9 9.8 %custom-call.64 = f32[1,128,128]{1,2,0:T(8,128)S(1)} custom-call(f32[1,128,128]{2,1,0:T(8,128)S(1)} %get-tuple-element.76), custom_call_target="InvertDiagBlocksLowerTriangular" | custom-call | tf_op jit(solution)/shard_map/jit(cholesky)/cholesky | solution.py:55
  322.2 12.1 %cholesky.487 = f32[128,128]{1,0:T(8,128)S(1)} custom-call(f32[128,128]{1,0:T(8,128)S(1)} %cholesky.594), custom_call_target="Cholesky" | custom-call | tf_op jit(solution)/shard_map/jit(cholesky)/cholesky | solution.py:55
  335.6 9.8 %custom-call.65 = f32[1,128,128]{1,2,0:T(8,128)S(1)} custom-call(f32[1,128,128]{2,1,0:T(8,128)S(1)} %get-tuple-element.73), custom_call_target="InvertDiagBlocksLowerTriangular" | custom-call | tf_op jit(solution)/shard_map/jit(cholesky)/cholesky | solution.py:55
  348.9 11.7 %cholesky.506 = f32[128,128]{1,0:T(8,128)S(1)} custom-call(f32[128,128]{1,0:T(8,128)S(1)} %cholesky.599), custom_call_target="Cholesky" | custom-call | tf_op jit(solution)/shard_map/jit(cholesky)/cholesky | solution.py:55
  362.0 9.8 %custom-call.66 = f32[1,128,128]{1,2,0:T(8,128)S(1)} custom-call(f32[1,128,128]{2,1,0:T(8,128)S(1)} %get-tuple-element.70), custom_call_target="InvertDiagBlocksLowerTriangular" | custom-call | tf_op jit(solution)/shard_map/jit(cholesky)/cholesky | solution.py:55
  375.3 11.7 %cholesky.526 = f32[128,128]{1,0:T(8,128)S(1)} custom-call(f32[128,128]{1,0:T(8,128)S(1)} %cholesky.604), custom_call_target="Cholesky" | custom-call | tf_op jit(solution)/shard_map/jit(cholesky)/cholesky | solution.py:55
  388.2 9.8 %custom-call.67 = f32[1,128,128]{1,2,0:T(8,128)S(1)} custom-call(f32[1,128,128]{2,1,0:T(8,128)S(1)} %get-tuple-element.67), custom_call_target="InvertDiagBlocksLowerTriangular" | custom-call | tf_op jit(solution)/shard_map/jit(cholesky)/cholesky | solution.py:55
  401.0 11.7 %cholesky.546 = f32[128,128]{1,0:T(8,128)S(1)} custom-call(f32[128,128]{1,0:T(8,128)S(1)} %cholesky.609), custom_call_target="Cholesky" | custom-call | tf_op jit(solution)/shard_map/jit(cholesky)/cholesky | solution.py:55
  414.1 9.9 %custom-call.68 = f32[1,128,128]{1,2,0:T(8,128)S(1)} custom-call(f32[1,128,128]{2,1,0:T(8,128)S(1)} %get-tuple-element.64), custom_call_target="InvertDiagBlocksLowerTriangular" | custom-call | tf_op jit(solution)/shard_map/jit(cholesky)/cholesky | solution.py:55
  426.7 11.7 %cholesky.564 = f32[128,128]{1,0:T(8,128)S(1)} custom-call(f32[128,128]{1,0:T(8,128)S(1)} %convolution_subtract_fusion.12), custom_call_target="Cholesky" | custom-call | tf_op jit(solution)/shard_map/jit(cholesky)/cholesky | solution.py:55
  452.0 23.3 %while.1 = (s32[]{:T(128)}, f32[1024,1024]{1,0:T(8,128)}, s32[8,2]{0,1:T(2,128)S(1)}, f32[8,128,128]{2,1,0:T(8,128)S(1)}, s32[]{:T(128)}) while((s32[]{:T(128)}, f32[1024,1024]{1,0:T(8,128)}, s32[8,2]{0,1:T(2,128)S(1)}, f32[8,128,128]{2,1,0:T(8,128)S(1)}, s32[]{:T(128)}) %tuple.73), condition=%wide.while_cond, body=%wide.while_body.sunk | while | flops 2 | bytes 131189 | solution.py:59
  475.3 79.0 %custom-call.69 = f32[8,128,128]{1,2,0:T(8,128)S(1)} custom-call(f32[8,128,128]{2,1,0:T(8,128)S(1)} %get-tuple-element.9), custom_call_target="InvertDiagBlocksLowerTriangular" | custom-call | tf_op jit(solution)/shard_map/triangular_solve | solution.py:59
  585.8 8.6 %convolution_subtract_fusion = f32[1408,128]{1,0:T(8,128)S(1)} fusion(f32[1408,768]{0,1:T(8,128)S(1)} %get-tuple-element.40, f32[1408,1024]{1,0:T(8,128)} %bitcast_dynamic-update-slice_fusion.2, f32[1024,1024]{1,0:T(8,128)} %get-tuple-element.147), kind=kOutput, calls=%fused_computation.22 | convolution fusion | flops 1661124608 | bytes 6160384 | tf_op jit(solution)/shard_map/triangular_solve | solution.py:59
  595.3 10.1 %convolution_subtract_fusion.4 = f32[1408,128]{1,0:T(8,128)S(1)} fusion(f32[1408,896]{0,1:T(8,128)S(1)} %get-tuple-element.36, f32[1408,1024]{1,0:T(8,128)} %bitcast_dynamic-update-slice_fusion.2, f32[1024,1024]{1,0:T(8,128)} %get-tuple-element.147), kind=kOutput, calls=%fused_computation.26 | convolution fusion | flops 1937948672 | bytes 6946816 | tf_op jit(solution)/shard_map/triangular_solve | solution.py:59
  617.8 9.0 %fusion.23 = f32[7,128,4,128]{3,1,2,0:T(8,128)S(1)} fusion(f32[1,8,1,128,4,1,128]{6,3,4,1,5,2,0:T(8,128)} %copy-done.2, f32[7,128,1024,1]{2,1,3,0:T(8,128)} %bitcast.188, f32[4,128,1024,1]{2,1,0,3:T(8,128)} %bitcast.191, f32[7,128,128]{2,1,0:T(8,128)S(1)} %constant_dynamic-slice_fusion.2, pred[4]{0:T(512)(128)(4,1)S(1)} %get-tuple-element.94), kind=kOutput, calls=%fused_computation.42 | convolution fusion | flops 5638062080 | bytes 9895940 | tf_op jit(solution)/shard_map/atk,bsk->atbs/dot_general | solution.py:66
  655.2 88.1 %all-to-all-done.1 = f32[16,1,65536]{2,1,0:T(1,128)} async-done(((f32[16,1,65536]{2,1,0:T(1,128)}), f32[16,1,65536]{2,1,0:T(1,128)}, u32[]{:S(2)}, u32[]{:S(2)}) %all-to-all-start.1) | async-done | bytes 4194336 | tf_op jit(solution)/shard_map/all_to_all | solution.py:124
  (151 shorter events, 202.7 us)
Async XLA Ops:
  8.0 83.8 %all-gather.5.cloned.1.call-start = ((), (), s32[]{:S(2)}) async-start(), calls=%async_computation.3 | async-start | bytes 8912896 | tf_op jit(solution)/shard_map/all_gather | solution.py:52
  9.9 1.3 copy-start.2
  94.3 1.9 copy-start
  98.8 6.9 slice-start
  98.8 7.7 %copy-start.4 = (s32[2,56]{1,0:T(2,128)S(1)}, s32[2,56]{1,0:T(2,128)}, u32[]{:S(2)}) copy-start(s32[2,56]{1,0:T(2,128)} %param.6) | copy-start | bytes 1348
  98.8 123.3 %all-to-all-start = ((f32[8,128,1024]{1,2,0:T(8,128)}), f32[8,128,1024]{1,2,0:T(8,128)}, u32[]{:S(2)}, u32[]{:S(2)}) async-start(f32[8,128,1024]{1,2,0:T(8,128)} %tile.9), calls=%async_computation | async-start | bytes 8388608 | tf_op jit(solution)/shard_map/all_to_all | solution.py:16
  105.7 87.7 %all-gather.7.cloned.1.call-start = ((), (), s32[]{:S(2)}) async-start(), calls=%async_computation.4 | async-start | bytes 2359296 | tf_op jit(solution)/shard_map/all_gather | solution.py:50
  222.0 421.0 %all-to-all-start.2 = ((s32[16,1,1]{2,1,0:T(1,128)}), s32[16,1,1]{2,1,0:T(1,128)S(1)}, u32[]{:S(2)}, u32[]{:S(2)}) async-start(s32[16,1,1]{2,1,0:T(1,128)} %copy.83), calls=%async_computation.2 | async-start | bytes 16384 | tf_op jit(solution)/shard_map/all_to_all | solution.py:125
  240.2 2.0 copy-start.1
  643.1 100.2 %all-to-all-start.1 = ((f32[16,1,65536]{2,1,0:T(1,128)}), f32[16,1,65536]{2,1,0:T(1,128)}, u32[]{:S(2)}, u32[]{:S(2)}) async-start(f32[16,1,65536]{2,1,0:T(1,128)} %copy.82), calls=%async_computation.1 | async-start | bytes 8388608 | tf_op jit(solution)/shard_map/all_to_all | solution.py:124
  655.2 98.9 %copy-start.3 = (f32[4,1,1,128,4,1,128]{6,5,4,3,2,1,0:T(1,128)S(1)}, f32[4,1,1,128,4,1,128]{6,5,4,3,2,1,0:T(1,128)}, u32[]{:S(2)}) copy-start(f32[4,1,1,128,4,1,128]{6,5,4,3,2,1,0:T(1,128)} %param.5) | copy-start | bytes 3145732
Sparse Core Ops, SparseCore 0:
  12.2 79.5 all-gather.4
Sparse Core Ops, SparseCore 1:
  108.5 84.8 all-gather.6
